TPU v7x, 512 devices: a whole 4x8x8 slice. The times are simulated.
512 devices in a mesh: row: 16 (over y, core), col: 32 (over z, x).
Axes of the slice: x: 4, y: 8, z: 8, core: 2. Of those that a mesh axis runs over, the one named last changes fastest.
Arguments:
- tokens: bfloat16 [1024, 8192], P('col', 'row'), may hold values from -6 to 6
- gate_weight: bfloat16 [8192, 16384], P('row', 'col'), may hold values from -0.09375 to 0.09375
- up_weight: bfloat16 [8192, 16384], P('row', 'col'), may hold values from -0.09375 to 0.09375
- down_weight: bfloat16 [16384, 8192], P('col', 'row'), may hold values from -0.0625 to 0.0625
- gate_mask: int32 [64, 128], P('row', 'col'), may hold values from 0 to 1, as said below
- up_mask: int32 [64, 128], P('row', 'col'), may hold values from 0 to 1, as said below
- down_mask: int32 [128, 64], P('col', 'row'), may hold values from 0 to 1, as said below
Outputs:
- mixed: bfloat16 [1024, 8192], P('col', 'row')
Inputs may be any that keep to these rules, and one draw needn't show every extreme that they name: `gate_mask`: each entry is 0 or 1; the share of ones differs from one block column of hidden units to another. `up_mask`: each entry is 0 or 1; the share of ones differs from one block column of hidden units to another. `down_mask`: each entry is 0 or 1; the share of ones differs from one block row of hidden units to another.
All inputs are finite; a program needn't handle non-finite values.
Results may differ from a plain program's by a relative error of at most 0.0049.
Values may be sent and summed in bfloat16 or wider, within the bound.
No kernel may reach another device: no remote copies, remote signals or barrier semaphores. Data moves between devices by JAX's collectives and lax.ppermute only.
A program may use at most 64 MiB of HBM per device.

v0:
```python
import jax
import jax.numpy as jnp
from jax import lax
from jax.sharding import PartitionSpec as P

BLK = 128


def widen(block_mask):
    rows_blocks, cols_blocks = block_mask.shape
    spread = jnp.broadcast_to(block_mask[:, None, :, None], (rows_blocks, BLK, cols_blocks, BLK))
    return spread.reshape(rows_blocks * BLK, cols_blocks * BLK).astype(jnp.bfloat16)


def swiglu(summed, hidden_cols):
    return (jax.nn.silu(summed[:, :hidden_cols]) * summed[:, hidden_cols:]).astype(jnp.bfloat16)


def on_device(tokens, gate_weight, up_weight, down_weight, gate_mask, up_mask, down_mask):
    hidden_cols = gate_weight.shape[1]
    both_weights = jnp.concatenate(
        [gate_weight * widen(gate_mask), up_weight * widen(up_mask)], axis=1
    )
    down_eff = down_weight * widen(down_mask)
    all_tokens = lax.all_gather(tokens, "col", axis=0, tiled=True)
    summed = lax.psum_scatter(
        jnp.dot(all_tokens, both_weights, preferred_element_type=jnp.float32),
        "row",
        scatter_dimension=0,
        tiled=True,
    )
    hidden_share = swiglu(summed, hidden_cols)
    hidden = lax.all_gather(hidden_share, "row", axis=0, tiled=True)
    out_rows = tokens.shape[0]
    partial_out = jnp.dot(hidden, down_eff, preferred_element_type=jnp.float32)
    whole_out = lax.psum(partial_out, "col")
    first_row = lax.axis_index("col") * out_rows
    mixed = lax.dynamic_slice_in_dim(whole_out, first_row, out_rows, 0)
    return mixed.astype(jnp.bfloat16)


def solution(mesh):
    placed = (
        P("col", "row"),
        P("row", "col"),
        P("row", "col"),
        P("col", "row"),
        P("row", "col"),
        P("row", "col"),
        P("col", "row"),
    )
    return jax.shard_map(
        on_device, mesh=mesh, in_specs=placed, out_specs=P("col", "row"), check_vma=False
    )
```

profile of v0, /device:TPU:8, one launch (start us, length us, event | category | flops | bytes accessed | tf_op | source)
XLA Modules:
  0.0 389.6 jit_solution(954516948314816408)
XLA Ops:
  6.5 0.0 all-gather.3.cloned.1.call-start
  6.5 0.7 all-gather.3.cloned.1.call-update
  7.3 0.0 reduce-scatter.4.cloned.1.call-start
  7.3 0.7 convert_element_type.29
  8.0 0.7 convert_element_type.27
  8.7 0.2 broadcast_in_dim.7
  8.9 0.2 broadcast_in_dim.6
  9.1 1.4 bitcast_multiply_fusion.2
  10.5 87.2 %all-gather.3.cloned.1.call-done = bf16[1024,512]{1,0:T(8,128)(2,1)} async-done(((bf16[32,512]{1,0:T(8,128)(2,1)}), bf16[1024,512]{1,0:T(8,128)(2,1)}) %all-gather.3.cloned.1.call-update) | async-done | bytes 1048592 | tf_op jit(solution)/shard_map/all_gather | solution.py:25
  97.7 4.5 %convolution_bitcast_fusion = f32[1024,1024]{0,1:T(8,128)} fusion(bf16[1024,512]{1,0:T(8,128)(2,1)} %all-gather.3.cloned.1.call-done, bf16[512,512]{1,0:T(8,128)(2,1)S(1)} %get-tuple-element.5, bf16[512,512]{1,0:T(8,128)(2,1)S(1)} %get-tuple-element.6), kind=kOutput, calls=%fused_computation | convolution fusion | flops 1075838976 | bytes 6291456 | tf_op jit(solution)/shard_map/dot_general | solution.py:27
  102.2 5.4 %copy.11 = f32[1024,1024]{1,0:T(8,128)} copy(f32[1024,1024]{0,1:T(8,128)} %convolution_bitcast_fusion) | data formatting | bytes 8388608
  107.5 0.0 copy-start.1
  107.5 0.0 copy-start
  107.5 0.0 reduce-scatter.4.cloned.1.call-update
  107.6 0.0 all-gather.5.cloned.1.call-start
  107.6 59.4 %reduce-scatter.4.cloned.1.call-done = f32[64,1024]{1,0:T(8,128)} async-done(((f32[1024,1024]{1,0:T(8,128)}), f32[64,1024]{1,0:T(8,128)}) %reduce-scatter.4.cloned.1.call-update) | async-done | bytes 262160 | tf_op jit(solution)/shard_map/reduce_scatter | solution.py:26
  167.1 1.6 fusion.5
  168.7 0.0 all-gather.5.cloned.1.call-update
  168.7 0.0 copy-done.1
  168.8 43.1 %all-gather.5.cloned.1.call-done = bf16[1024,512]{1,0:T(8,128)(2,1)} async-done(((bf16[64,512]{1,0:T(8,128)(2,1)}), bf16[1024,512]{1,0:T(8,128)(2,1)}) %all-gather.5.cloned.1.call-update) | async-done | bytes 1048592 | tf_op jit(solution)/shard_map/all_gather | solution.py:33
  211.9 0.2 broadcast_in_dim.8
  212.1 0.0 copy-done
  212.1 1.9 fusion.3
  214.1 168.3 %all-reduce.1 = bf16[1024,512]{1,0:T(8,128)(2,1)S(1)} all-reduce(f32[1024,512]{1,0:T(8,128)S(1)} %fusion.3), channel_id=1, replica_groups=mesh['row'=16,'col'=32] {'col'}, use_global_device_ids=true, to_apply=%region_1.2 | all-reduce | flops 524288 | bytes 3145728 | tf_op jit(solution)/shard_map/psum | solution.py:36
  382.4 0.6 dynamic-slice_convert_fusion
  (1 shorter events, 0.0 us)
Async XLA Ops:
  6.5 91.2 %all-gather.3.cloned.1.call-start = ((), (), s32[]{:S(2)}) async-start(), calls=%async_computation.1 | async-start | bytes 1081344 | tf_op jit(solution)/shard_map/all_gather | solution.py:25
  7.3 159.8 %reduce-scatter.4.cloned.1.call-start = ((), (), s32[]{:S(2)}) async-start(), calls=%async_computation.3 | async-start | bytes 4456448 | tf_op jit(solution)/shard_map/reduce_scatter | solution.py:26
  107.5 61.2 %copy-start.1 = (s32[4,4]{1,0:T(4,128)S(1)}, s32[4,4]{1,0:T(4,128)}, u32[]{:S(2)}) copy-start(s32[4,4]{1,0:T(4,128)} %param.13) | copy-start | bytes 196
  107.5 104.6 %copy-start = (bf16[512,512]{1,0:T(8,128)(2,1)S(1)}, bf16[512,512]{1,0:T(8,128)(2,1)}, u32[]{:S(2)}) copy-start(bf16[512,512]{1,0:T(8,128)(2,1)} %param.10) | copy-start | bytes 1572868
  107.6 104.3 %all-gather.5.cloned.1.call-start = ((), (), s32[]{:S(2)}) async-start(), calls=%async_computation.2 | async-start | bytes 1114112 | tf_op jit(solution)/shard_map/all_gather | solution.py:33
Sparse Core Ops, SparseCore 0:
  10.5 87.1 all-gather.2
  107.7 59.3 reduce-scatter.3
  169.2 42.6 all-gather.4
where the time goes:
time: 390 us
  waiting for transfers between devices  191 us (49%)
  blocking collectives  168 us (43%)
  between operations  13.2 us (3%)
  local copies, waits for them, and re-layouts  6.63 us (2%)
  matrix products  6.41 us (2%)
  other arithmetic  4.37 us (1%)
    psum x1, blocking collectives, on_device(): whole_out = lax.psum(partial_out, 'col')  168 us
    all_gather x1, waiting for transfers between devices, on_device(): all_tokens = lax.all_gather(tokens, 'col', axis=0, tiled=True)  87.2 us
    reduce_scatter x1, waiting for transfers between devices, on_device(): lax.psum_scatter(jnp.dot(all_tokens, both_weights, preferred_element_type...  59.4 us
    all_gather x1, waiting for transfers between devices, on_device(): hidden = lax.all_gather(hidden_share, 'row', axis=0, tiled=True)  43.1 us
  transfers between devices with their start and end apart: 3, of which 3 were waited for; matrix products, arithmetic and copies ran while one was open for 1% of the time, Pallas kernels for 0%

commit v1 on v0

--- a/solution.py
+++ b/solution.py
@@ -33,7 +33,11 @@
     hidden = lax.all_gather(hidden_share, "row", axis=0, tiled=True)
     out_rows = tokens.shape[0]
     partial_out = jnp.dot(hidden, down_eff, preferred_element_type=jnp.float32)
-    whole_out = lax.psum(partial_out, "col")
+    whole_out = partial_out
+    for hop in (1, 2, 4, 8, 16):
+        whole_out = whole_out + lax.ppermute(
+            whole_out, "col", [(dev, dev ^ hop) for dev in range(32)]
+        )
     first_row = lax.axis_index("col") * out_rows
     mixed = lax.dynamic_slice_in_dim(whole_out, first_row, out_rows, 0)
     return mixed.astype(jnp.bfloat16)

time: 390 us -> 565 us (1.45)
  the two profiles are of different devices: /device:TPU:8 before, /device:TPU:1 now
where the time goes in v1:
time: 565 us
  waiting for transfers between devices  507 us (90%)
  starting transfers between devices  23.9 us (4%)
  between operations  13.2 us (2%)
  other arithmetic  7.73 us (1%)
  matrix products  6.42 us (1%)
  local copies, waits for them, and re-layouts  6 us (1%)
    ppermute x5, waiting for transfers between devices, on_device(): lax.ppermute(whole_out, 'col', [(dev, dev ^ hop) for dev in range(32)])  315 us
    all_gather x1, waiting for transfers between devices, on_device(): all_tokens = lax.all_gather(tokens, 'col', axis=0, tiled=True)  82.7 us
    reduce_scatter x1, waiting for transfers between devices, on_device(): lax.psum_scatter(jnp.dot(all_tokens, both_weights, preferred_element_type...  66.2 us
    all_gather x1, waiting for transfers between devices, on_device(): hidden = lax.all_gather(hidden_share, 'row', axis=0, tiled=True)  42.4 us
    ppermute x5, starting transfers between devices, on_device(): lax.ppermute(whole_out, 'col', [(dev, dev ^ hop) for dev in range(32)])  23.9 us
  transfers between devices with their start and end apart: 8, of which 8 were waited for; matrix products, arithmetic and copies ran while one was open for 1% of the time, Pallas kernels for 0%

profile of v1, /device:TPU:1, one launch (start us, length us, event | category | flops | bytes accessed | tf_op | source)
XLA Modules:
  0.0 564.6 jit_solution(14110691006836552139)
XLA Ops:
  6.5 0.7 all-gather.3.cloned.1.call-update
  7.3 0.0 reduce-scatter.4.cloned.1.call-start
  7.3 0.7 convert_element_type.27
  8.0 0.7 convert_element_type.29
  8.7 0.2 broadcast_in_dim.6
  8.9 0.2 broadcast_in_dim.7
  9.1 1.4 bitcast_multiply_fusion.2
  10.5 82.7 %all-gather.3.cloned.1.call-done = bf16[1024,512]{1,0:T(8,128)(2,1)} async-done(((bf16[32,512]{1,0:T(8,128)(2,1)}), bf16[1024,512]{1,0:T(8,128)(2,1)}) %all-gather.3.cloned.1.call-update) | async-done | bytes 1048592 | tf_op jit(solution)/shard_map/all_gather | solution.py:25
  93.2 4.5 convolution_bitcast_fusion
  97.7 5.4 copy.11
  103.1 0.0 reduce-scatter.4.cloned.1.call-update
  103.1 0.0 all-gather.5.cloned.1.call-start
  103.1 66.2 %reduce-scatter.4.cloned.1.call-done = f32[64,1024]{1,0:T(8,128)} async-done(((f32[1024,1024]{1,0:T(8,128)}), f32[64,1024]{1,0:T(8,128)}) %reduce-scatter.4.cloned.1.call-update) | async-done | bytes 262160 | tf_op jit(solution)/shard_map/reduce_scatter | solution.py:26
  169.4 1.6 fusion.5
  171.0 42.4 %all-gather.5.cloned.1.call-done = bf16[1024,512]{1,0:T(8,128)(2,1)} async-done(((bf16[64,512]{1,0:T(8,128)(2,1)}), bf16[1024,512]{1,0:T(8,128)(2,1)}) %all-gather.5.cloned.1.call-update) | async-done | bytes 1048592 | tf_op jit(solution)/shard_map/all_gather | solution.py:33
  213.5 0.2 broadcast_in_dim.8
  213.7 1.9 fusion.3
  215.7 3.1 collective-permute-start
  218.8 45.7 %collective-permute-done = f32[1024,512]{1,0:T(8,128)S(1)} collective-permute-done((f32[1024,512]{1,0:T(8,128)S(1)}, f32[1024,512]{1,0:T(8,128)S(1)}, u32[]{:S(2)}, u32[]{:S(2)}) %collective-permute-start) | collective-permute-done | bytes 2097184 | tf_op jit(solution)/shard_map/ppermute | solution.py:38
  264.5 0.5 add.25
  264.9 4.6 collective-permute-start.1
  269.5 44.8 %collective-permute-done.1 = f32[1024,512]{1,0:T(8,128)S(1)} collective-permute-done((f32[1024,512]{1,0:T(8,128)S(1)}, f32[1024,512]{1,0:T(8,128)S(1)}, u32[]{:S(2)}, u32[]{:S(2)}) %collective-permute-start.1) | collective-permute-done | bytes 2097184 | tf_op jit(solution)/shard_map/ppermute | solution.py:38
  314.4 0.5 add.26
  314.9 3.3 collective-permute-start.2
  318.1 43.8 %collective-permute-done.2 = f32[1024,512]{1,0:T(8,128)S(1)} collective-permute-done((f32[1024,512]{1,0:T(8,128)S(1)}, f32[1024,512]{1,0:T(8,128)S(1)}, u32[]{:S(2)}, u32[]{:S(2)}) %collective-permute-start.2) | collective-permute-done | bytes 2097184 | tf_op jit(solution)/shard_map/ppermute | solution.py:38
  361.9 0.5 add.27
  362.4 4.3 collective-permute-start.3
  366.8 89.9 %collective-permute-done.3 = f32[1024,512]{1,0:T(8,128)S(1)} collective-permute-done((f32[1024,512]{1,0:T(8,128)S(1)}, f32[1024,512]{1,0:T(8,128)S(1)}, u32[]{:S(2)}, u32[]{:S(2)}) %collective-permute-start.3) | collective-permute-done | bytes 2097184 | tf_op jit(solution)/shard_map/ppermute | solution.py:38
  456.7 0.5 add.28
  457.2 8.6 %collective-permute-start.4 = (f32[1024,512]{1,0:T(8,128)S(1)}, f32[1024,512]{1,0:T(8,128)}, u32[]{:S(2)}, u32[]{:S(2)}) collective-permute-start(f32[1024,512]{1,0:T(8,128)S(1)} %add.28), channel_id=1, source_target_pairs={{0,16},{1,17},{2,18},{3,19},{4,20},{5,21},{6,22},{7,23},{8,24},{9,... | collective-permute-start | bytes 6291464 | tf_op jit(solution)/shard_map/ppermute | solution.py:38
  465.7 90.9 %collective-permute-done.4 = f32[1024,512]{1,0:T(8,128)} collective-permute-done((f32[1024,512]{1,0:T(8,128)S(1)}, f32[1024,512]{1,0:T(8,128)}, u32[]{:S(2)}, u32[]{:S(2)}) %collective-permute-start.4) | collective-permute-done | bytes 2097184 | tf_op jit(solution)/shard_map/ppermute | solution.py:38
  556.6 1.5 fusion.6
  (7 shorter events, 0.0 us)
Async XLA Ops:
  6.5 86.7 %all-gather.3.cloned.1.call-start = ((), (), s32[]{:S(2)}) async-start(), calls=%async_computation.1 | async-start | bytes 1081344 | tf_op jit(solution)/shard_map/all_gather | solution.py:25
  7.3 162.1 %reduce-scatter.4.cloned.1.call-start = ((), (), s32[]{:S(2)}) async-start(), calls=%async_computation.3 | async-start | bytes 4456448 | tf_op jit(solution)/shard_map/reduce_scatter | solution.py:26
  103.1 68.0 %copy-start.1 = (s32[4,4]{1,0:T(4,128)S(1)}, s32[4,4]{1,0:T(4,128)}, u32[]{:S(2)}) copy-start(s32[4,4]{1,0:T(4,128)} %param.13) | copy-start | bytes 196
  103.1 110.7 %copy-start = (bf16[512,512]{1,0:T(8,128)(2,1)S(1)}, bf16[512,512]{1,0:T(8,128)(2,1)}, u32[]{:S(2)}) copy-start(bf16[512,512]{1,0:T(8,128)(2,1)} %param.10) | copy-start | bytes 1572868
  103.1 110.4 %all-gather.5.cloned.1.call-start = ((), (), s32[]{:S(2)}) async-start(), calls=%async_computation.2 | async-start | bytes 1114112 | tf_op jit(solution)/shard_map/all_gather | solution.py:33
  215.7 48.8 %collective-permute-start = (f32[1024,512]{1,0:T(8,128)S(1)}, f32[1024,512]{1,0:T(8,128)S(1)}, u32[]{:S(2)}, u32[]{:S(2)}) collective-permute-start(f32[1024,512]{1,0:T(8,128)S(1)} %fusion.3), channel_id=1, source_target_pairs={{0,1},{1,0},{2,3},{3,2},{4,5},{5,4},{6,7},{7,6},{8,9},{9,8},{10,11... | collective-permute-start | bytes 6291464 | tf_op jit(solution)/shard_map/ppermute | solution.py:38
  264.9 49.4 %collective-permute-start.1 = (f32[1024,512]{1,0:T(8,128)S(1)}, f32[1024,512]{1,0:T(8,128)S(1)}, u32[]{:S(2)}, u32[]{:S(2)}) collective-permute-start(f32[1024,512]{1,0:T(8,128)S(1)} %add.25), channel_id=1, source_target_pairs={{0,2},{1,3},{2,0},{3,1},{4,6},{5,7},{6,4},{7,5},{8,10},{9,11},{10,... | collective-permute-start | bytes 6291464 | tf_op jit(solution)/shard_map/ppermute | solution.py:38
  314.9 47.1 %collective-permute-start.2 = (f32[1024,512]{1,0:T(8,128)S(1)}, f32[1024,512]{1,0:T(8,128)S(1)}, u32[]{:S(2)}, u32[]{:S(2)}) collective-permute-start(f32[1024,512]{1,0:T(8,128)S(1)} %add.26), channel_id=1, source_target_pairs={{0,4},{1,5},{2,6},{3,7},{4,0},{5,1},{6,2},{7,3},{8,12},{9,13},{10,... | collective-permute-start | bytes 6291464 | tf_op jit(solution)/shard_map/ppermute | solution.py:38
  362.4 94.3 %collective-permute-start.3 = (f32[1024,512]{1,0:T(8,128)S(1)}, f32[1024,512]{1,0:T(8,128)S(1)}, u32[]{:S(2)}, u32[]{:S(2)}) collective-permute-start(f32[1024,512]{1,0:T(8,128)S(1)} %add.27), channel_id=1, source_target_pairs={{0,8},{1,9},{2,10},{3,11},{4,12},{5,13},{6,14},{7,15},{8,0},{9,1},... | collective-permute-start | bytes 6291464 | tf_op jit(solution)/shard_map/ppermute | solution.py:38
  457.2 99.5 %collective-permute-start.4 = (f32[1024,512]{1,0:T(8,128)S(1)}, f32[1024,512]{1,0:T(8,128)}, u32[]{:S(2)}, u32[]{:S(2)}) collective-permute-start(f32[1024,512]{1,0:T(8,128)S(1)} %add.28), channel_id=1, source_target_pairs={{0,16},{1,17},{2,18},{3,19},{4,20},{5,21},{6,22},{7,23},{8,24},{9,... | collective-permute-start | bytes 6291464 | tf_op jit(solution)/shard_map/ppermute | solution.py:38
Sparse Core Ops, SparseCore 0:
  10.5 82.6 all-gather.2
  103.2 66.1 reduce-scatter.3
  171.5 41.9 all-gather.4
